TPU v7x, 128 devices: a whole 4x4x4 slice. The times are simulated.
128 devices in a mesh: group: 16 (over x, z), mp: 8 (over y, core).
Axes of the slice: x: 4, y: 4, z: 4, core: 2. Of those that a mesh axis runs over, the one named last changes fastest.
Arguments:
- stream: bfloat16 [8192, 3584], P('group', 'mp'), may hold values from -6 to 6
- prenorm_gain: float32 [3584], replicated, may hold values from 0.25 to 12
- query_weight: bfloat16 [3584, 4096], P(None, 'mp'), may hold values from -0.09375 to 0.09375
- key_weight: bfloat16 [3584, 2048], P(None, 'mp'), may hold values from -0.09375 to 0.09375
- value_weight: bfloat16 [3584, 2048], P(None, 'mp'), may hold values from -0.09375 to 0.09375
- output_weight: bfloat16 [4096, 3584], P('mp'), may hold values from -0.09375 to 0.09375
- adapter_down_rows: bfloat16 [64, 16, 3584], P('group', None, 'mp'), may hold values from -0.09375 to 0.09375
- adapter_up_query: bfloat16 [64, 16, 4096], P('group', None, 'mp'), may hold values from -1.5 to 1.5
- request_adapter: int32 [16, 4], replicated, may hold values from 0 to 63
- adapter_row_index: int32 [64], replicated, may hold values from 0 to 63, each once
- request_token_length: int32 [16, 4], replicated, may hold values from 1 to 256, 512 in all within a row
- continues_previous: int32 [16], replicated, may hold values from 0 to 1, as said below
- request_cache_block: int32 [16, 4], replicated, may hold values from 0 to 31, as said below
- cached_length: int32 [16, 4], replicated, may hold values from 1 to 256
- cached_rotated_keys: bfloat16 [32, 256, 2048], P('group', None, 'mp'), may hold values from -6 to 6
- cached_value_rows: bfloat16 [32, 256, 2048], P('group', None, 'mp'), may hold values from -6 to 6
Outputs:
- attn_out: bfloat16 [8192, 3584], P('group', 'mp')
Inputs may be any that keep to these rules, and one draw needn't show every extreme that they name: `continues_previous`: the first group has 0; some group has 1. `request_cache_block`: the owner of block b is group b // 2; blocks may be shared by requests.
All inputs are finite; a program needn't handle non-finite values.
Results may differ from a plain program's by a relative error of at most 0.017.
The roundings to bfloat16 on the way count: a program that leaves them out, or rounds other values in their place, can miss the bound.
Values may be sent and summed in bfloat16 or wider, within the bound.
No kernel may reach another device: no remote copies, remote signals or barrier semaphores. Data moves between devices by JAX's collectives and lax.ppermute only.
A program may use at most 128 MiB of HBM per device.

v0:
```python
import jax
import jax.numpy as jnp
from jax import lax
from jax.sharding import PartitionSpec as P

HEAD_WIDTH = 256
REQS = 4
adapter_scale = 2.0


def shifted(value, axis, steps):
    count = lax.axis_size(axis)
    first, last = (max(0, -steps), min(count, count - steps))
    return lax.ppermute(value, axis, [(source, source + steps) for source in range(first, last)])


def rotate(values, position, head_size):
    count = values.shape[0]
    shaped = values.reshape(count, -1, head_size)
    half = head_size // 2
    freq = 10000.0 ** (-jnp.arange(half, dtype=jnp.float32) / half)
    angle = position[:, None, None] * freq[None, None, :]
    cosine = jnp.cos(angle)
    sine = jnp.sin(angle)
    first = shaped[..., :half]
    second = shaped[..., half:]
    turned = jnp.concatenate(
        [first * cosine - second * sine, second * cosine + first * sine], axis=-1
    )
    return turned.reshape(count, -1)


def layout(lengths, cached, split_flag, prev_len, count):
    ends = jnp.cumsum(lengths)
    starts = ends - lengths
    place = jnp.arange(count, dtype=jnp.int32)
    member = ((place[:, None] >= starts[None, :]) & (place[:, None] < ends[None, :])).astype(
        jnp.int32
    )
    request = jnp.sum(member * jnp.arange(lengths.shape[0], dtype=jnp.int32)[None, :], axis=1)
    offset = place - jnp.sum(member * starts[None, :], axis=1)
    extra = jnp.where(request == 0, split_flag * prev_len, 0)
    position = jnp.sum(member * cached[None, :], axis=1) + extra + offset
    return (member, request, position.astype(jnp.float32))


def attend(
    query_vectors,
    keys,
    values,
    prev_keys,
    prev_values,
    cache_keys,
    cache_values,
    request,
    cached,
    split_flag,
    prev_len,
    head_size,
):
    count = query_vectors.shape[0]
    kv_heads = keys.shape[1] // head_size
    ratio = query_vectors.shape[1] // keys.shape[1]
    block = cache_keys.shape[1]
    slots = cache_keys.shape[0] * block
    every_key = jnp.concatenate([cache_keys.reshape(slots, -1), prev_keys, keys], 0).reshape(
        -1, kv_heads, head_size
    )
    every_value = jnp.concatenate(
        [cache_values.reshape(slots, -1), prev_values, values], 0
    ).reshape(-1, kv_heads, head_size)
    slot_req = jnp.arange(slots, dtype=jnp.int32) // block
    slot_col = jnp.arange(slots, dtype=jnp.int32) % block
    cache_ok = (request[:, None] == slot_req[None, :]) & (
        slot_col[None, :] < cached[slot_req][None, :]
    )
    place = jnp.arange(count, dtype=jnp.int32)
    prev_ok = (split_flag == 1) & (request[:, None] == 0) & (place[None, :] >= count - prev_len)
    own_ok = (request[:, None] == request[None, :]) & (place[None, :] <= place[:, None])
    allowed = jnp.concatenate([cache_ok, prev_ok, own_ok], 1)
    grouped = query_vectors.reshape(count, kv_heads, ratio, head_size)
    scores = jnp.einsum(
        "tkrd,skd->krts", grouped, every_key, preferred_element_type=jnp.float32
    ) * head_size ** (-0.5)
    scores = jnp.where(allowed[None, None], scores, jnp.float32(-1e30))
    top = jnp.max(scores, axis=-1, keepdims=True)
    weights = jnp.exp(scores - top)
    total = jnp.sum(weights, axis=-1)
    numer = jnp.einsum(
        "krts,skd->tkrd",
        weights.astype(jnp.bfloat16),
        every_value,
        preferred_element_type=jnp.float32,
    )
    result = numer / jnp.transpose(total, (2, 0, 1))[..., None]
    return result.reshape(count, -1).astype(jnp.bfloat16)


def on_device(
    stream,
    prenorm_gain,
    query_weight,
    key_weight,
    value_weight,
    output_weight,
    adapter_down_rows,
    adapter_up_query,
    request_adapter,
    adapter_row_index,
    request_token_length,
    continues_previous,
    request_cache_block,
    cached_length,
    cached_rotated_keys,
    cached_value_rows,
):
    count = stream.shape[0]
    width = stream.shape[1]
    group_at = lax.axis_index("group")
    model_at = lax.axis_index("mp")
    whole = lax.all_gather(stream, "mp", axis=1, tiled=True)
    wide = whole.astype(jnp.float32)
    normalized_input = (
        wide * lax.rsqrt(jnp.mean(wide * wide, axis=1, keepdims=True) + 1e-06) * prenorm_gain
    ).astype(jnp.bfloat16)
    normed_part = lax.dynamic_slice_in_dim(normalized_input, model_at * width, width, 1)
    before = jnp.maximum(group_at - 1, 0)
    lengths = request_token_length[group_at]
    cached = cached_length[group_at]
    split_flag = continues_previous[group_at]
    prev_len = request_token_length[before, REQS - 1]
    member, request, position = layout(lengths, cached, split_flag, prev_len, count)
    wanted = adapter_row_index[request_adapter[group_at]]
    pieces = (
        lax.all_gather(adapter_down_rows, "group", axis=0, tiled=True),
        lax.all_gather(adapter_up_query, "group", axis=0, tiled=True),
    )
    stored = jnp.arange(pieces[0].shape[0], dtype=jnp.int32)
    onehot = (wanted[:, None] == stored[None, :]).astype(jnp.bfloat16)
    new_down = jnp.einsum("rj,jkd->rkd", onehot, pieces[0], preferred_element_type=jnp.float32)
    new_up = jnp.einsum("rj,jkd->rkd", onehot, pieces[1], preferred_element_type=jnp.float32)
    chosen_down = new_down.astype(jnp.bfloat16)
    chosen_up = new_up.astype(jnp.bfloat16)
    rank_index = adapter_down_rows.shape[1]
    partial_low = jnp.einsum(
        "td,rkd->trk", normed_part, chosen_down, preferred_element_type=jnp.float32
    ).reshape(count, REQS * rank_index)
    low = lax.psum(partial_low, "mp").astype(jnp.bfloat16)
    own_columns = jnp.repeat(member, rank_index, axis=1).astype(jnp.bfloat16)
    query_update = jnp.dot(
        low * own_columns,
        chosen_up.reshape(REQS * rank_index, -1),
        preferred_element_type=jnp.float32,
    )
    query_vectors = (
        jnp.dot(normalized_input, query_weight, preferred_element_type=jnp.float32)
        + adapter_scale * query_update
    )
    query_vectors = rotate(query_vectors, position, HEAD_WIDTH).astype(jnp.bfloat16)
    keys = rotate(
        jnp.dot(normalized_input, key_weight, preferred_element_type=jnp.float32),
        position,
        HEAD_WIDTH,
    ).astype(jnp.bfloat16)
    values = jnp.dot(normalized_input, value_weight, preferred_element_type=jnp.float32).astype(
        jnp.bfloat16
    )
    prev_keys, prev_values = shifted((keys, values), "group", 1)
    blocks = request_cache_block[group_at]
    pieces = (
        lax.all_gather(cached_rotated_keys, "group", axis=0, tiled=True),
        lax.all_gather(cached_value_rows, "group", axis=0, tiled=True),
    )
    stored = jnp.arange(pieces[0].shape[0], dtype=jnp.int32)
    onehot = (blocks[:, None] == stored[None, :]).astype(jnp.bfloat16)
    new_keys = jnp.einsum("rj,jcd->rcd", onehot, pieces[0], preferred_element_type=jnp.float32)
    new_values = jnp.einsum("rj,jcd->rcd", onehot, pieces[1], preferred_element_type=jnp.float32)
    cache_keys = new_keys.astype(jnp.bfloat16)
    cache_values = new_values.astype(jnp.bfloat16)
    attended = attend(
        query_vectors,
        keys,
        values,
        prev_keys,
        prev_values,
        cache_keys,
        cache_values,
        request,
        cached,
        split_flag,
        prev_len,
        HEAD_WIDTH,
    )
    partial_out = jnp.dot(attended, output_weight, preferred_element_type=jnp.float32)
    return lax.psum_scatter(partial_out.astype(jnp.bfloat16), "mp", scatter_dimension=1, tiled=True)


def solution(mesh):
    placed = (
        P("group", "mp"),
        P(),
        P(None, "mp"),
        P(None, "mp"),
        P(None, "mp"),
        P("mp", None),
        P("group", None, "mp"),
        P("group", None, "mp"),
        P(),
        P(),
        P(),
        P(),
        P(),
        P(),
        P("group", None, "mp"),
        P("group", None, "mp"),
    )
    return jax.shard_map(
        on_device, mesh=mesh, in_specs=placed, out_specs=P("group", "mp"), check_vma=False
    )
```

profile of v0, /device:TPU:0, one launch (start us, length us, event | category | flops | bytes accessed | tf_op | source)
XLA Modules:
  0.0 254.0 jit_solution(16617972660007501374)
XLA Ops:
  13.4 26.9 %all_gather.18 = bf16[64,16,448]{2,1,0:T(8,128)(2,1)S(1)} all-gather(bf16[4,16,448]{2,1,0:T(8,128)(2,1)} %param.22), channel_id=1, replica_groups=mesh['group'=16,'mp'=8] {'group'}, dimensions={0}, use_global_device_ids=true | all-gather | bytes 974848 | tf_op jit(solution)/shard_map/all_gather | solution.py:135
  40.9 2.6 %compare_select_fusion.1 = s32[1024,1]{0,1:T(1,128)S(1)} fusion(s32[]{:T(128)} %bitcast.7, s32[]{:T(128)} %bitcast.8, s32[]{:T(128)} %bitcast.10, s32[]{:T(128)} %bitcast.9), kind=kLoop, calls=%fused_computation.71 | loop fusion | flops 17408 | bytes 4112 | tf_op jit(solution)/shard_map/gather | solution.py:75
  49.5 1.8 multiply_cosine_fusion
  54.9 2.4 convolution_convert_fusion.2
  57.4 28.5 %all-gather.7.cloned.1.call-done = bf16[512,3584]{0,1:T(8,128)(2,1)} async-done(((bf16[512,448]{0,1:T(8,128)(2,1)}), bf16[512,3584]{0,1:T(8,128)(2,1)}) %all-gather.7.cloned.1.call-update) | async-done | bytes 3670032 | tf_op jit(solution)/shard_map/all_gather | solution.py:121
  85.8 3.0 %fusion.2 = f32[512]{0:T(512)S(1)} fusion(bf16[512,3584]{0,1:T(8,128)(2,1)} %all-gather.7.cloned.1.call-done), kind=kLoop, calls=%fused_computation.7 | loop fusion | flops 5504512 | bytes 3672064 | tf_op jit(solution)/shard_map/reduce_sum | solution.py:124
  90.6 1.8 copy-done.2
  92.4 1.9 convolution_convert_fusion.1
  96.1 4.2 %collective-permute-start = (bf16[512,256]{1,0:T(8,128)(2,1)}, bf16[512,256]{1,0:T(8,128)(2,1)}, u32[]{:S(2)}, u32[]{:S(2)}) collective-permute-start(bf16[512,256]{1,0:T(8,128)(2,1)} %convolution_convert_fusion.1), channel_id=1, source_target_pairs={{0,8},{8,16},{16,24},{24,32},{32,40},{40,48},{48,56},{56,64},{64,7... | collective-permute-start | bytes 786440 | tf_op jit(solution)/shard_map/ppermute | solution.py:14
  100.2 3.8 %convolution_bitcast_fusion = f32[512,1,256]{0,2,1:T(8,128)S(1)} fusion(bf16[512,3584]{0,1:T(8,128)(2,1)} %copy-done.2, bf16[3584,256]{1,0:T(8,128)(2,1)} %param.19), kind=kOutput, calls=%fused_computation.26 | convolution fusion | flops 939524096 | bytes 6029312 | tf_op jit(solution)/shard_map/dot_general | solution.py:161
  107.7 3.4 %collective-permute-start.1 = (bf16[512,256]{0,1:T(8,128)(2,1)}, bf16[512,256]{0,1:T(8,128)(2,1)}, u32[]{:S(2)}, u32[]{:S(2)}) collective-permute-start(bf16[512,256]{0,1:T(8,128)(2,1)} %maximum_bitcast_fusion.6), channel_id=1, source_target_pairs={{0,8},{8,16},{16,24},{24,32},{32,40},{40,48},{48,56},{56,64},{64,7... | collective-permute-start | bytes 786440 | tf_op jit(solution)/shard_map/ppermute | solution.py:14
  112.3 26.0 %all-reduce.1 = bf16[512,64]{0,1:T(8,128)(2,1)S(1)} all-reduce(f32[512,64]{0,1:T(8,128)S(1)} %bitcast.101), channel_id=1, replica_groups=mesh['group'=16,'mp'=8] {'mp'}, use_global_device_ids=true, to_apply=%region_5.6 | all-reduce | flops 32768 | bytes 196608 | tf_op jit(solution)/shard_map/psum | solution.py:148
  138.4 5.3 %fusion.82 = f32[512,512]{0,1:T(8,128)S(1)} fusion(bf16[512,3584]{0,1:T(8,128)(2,1)} %copy-done.2, bf16[3584,512]{1,0:T(8,128)(2,1)} %param.18), kind=kOutput, calls=%fused_computation.129 | convolution fusion | flops 1879048192 | bytes 8388608 | tf_op jit(solution)/shard_map/dot_general | solution.py:156
  146.4 2.1 copy.62
  148.5 2.2 subtract_convert_fusion
  150.6 1.8 copy.46
  154.3 4.6 %fusion.18 = bf16[4,256,256]{2,0,1:T(4,128)(2,1)S(1)} fusion(bf16[32,256,256]{2,1,0:T(8,128)(2,1)} %all-gather.5.cloned.1.call-done, s32[4]{0:T(128)S(1)} %dynamic-slice_reduce_fusion.1), kind=kOutput, calls=%fused_computation.24 | convolution fusion | flops 17039488 | bytes 4718608 | tf_op jit(solution)/shard_map/rj,jcd->rcd/dot_general | solution.py:177
  160.0 35.3 %all-gather.9.cloned.1.call-done = bf16[32,256,256]{2,1,0:T(8,128)(2,1)} async-done(((bf16[2,256,256]{2,1,0:T(8,128)(2,1)}), bf16[32,256,256]{2,1,0:T(8,128)(2,1)}) %all-gather.9.cloned.1.call-update) | async-done | bytes 4194320 | tf_op jit(solution)/shard_map/all_gather | solution.py:171
  195.3 4.7 %fusion.21 = bf16[4,256,256]{2,0,1:T(4,128)(2,1)S(1)} fusion(bf16[32,256,256]{2,1,0:T(8,128)(2,1)} %all-gather.9.cloned.1.call-done, s32[4]{0:T(128)S(1)} %dynamic-slice_reduce_fusion.1), kind=kOutput, calls=%fused_computation.25 | convolution fusion | flops 17039488 | bytes 4718608 | tf_op jit(solution)/shard_map/rj,jcd->rcd/dot_general | solution.py:176
  200.1 1.8 fusion.5
  201.9 2.2 fusion
  204.2 2.8 %divide_convert_fusion = bf16[512,1,2,256]{0,3,2,1:T(8,128)(2,1)S(1)} fusion(f32[2048,512,2]{1,0,2:T(8,128)S(1)} %get-tuple-element.25, f32[2,512]{1,0:T(2,128)S(1)} %get-tuple-element.24, pred[512,2048]{0,1:T(8,128)(4,1)S(1)} %pad_add_fusion, bf16[512,256]{0,1:T(8,128)(2,1)S(1)} %copy-done.4, bf16[512,256]{0,1:T(8,128)(2,1)S(1)} %copy-done.6, ...), kind=kOutput, calls=%fused_computation.43 | convolution fusion | flops 1085800448 | bytes 11018240 | tf_op jit(solution)/shard_map/krts,skd->tkrd/dot_general | solution.py:89
  207.0 3.9 %convolution_convert_fusion = bf16[512,3584]{0,1:T(8,128)(2,1)} fusion(bf16[512,512]{0,1:T(8,128)(2,1)S(1)} %bitcast.107, bf16[512,3584]{1,0:T(8,128)(2,1)S(1)} %copy-done.11), kind=kOutput, calls=%fused_computation.11 | convolution fusion | flops 1880883200 | bytes 7864320 | tf_op jit(solution)/shard_map/dot_general | solution.py:194
  210.9 36.5 %reduce-scatter.2.cloned.1.call-done = bf16[512,448]{0,1:T(8,128)(2,1)} async-done(((bf16[512,3584]{0,1:T(8,128)(2,1)}), bf16[512,448]{0,1:T(8,128)(2,1)}) %reduce-scatter.2.cloned.1.call-update) | async-done | bytes 458768 | tf_op jit(solution)/shard_map/reduce_scatter | solution.py:195
  (78 shorter events, 28.4 us)
Async XLA Ops:
  6.5 85.8 %copy-start = (bf16[3584,256]{1,0:T(8,128)(2,1)S(1)}, bf16[3584,256]{1,0:T(8,128)(2,1)}, u32[]{:S(2)}) copy-start(bf16[3584,256]{1,0:T(8,128)(2,1)} %param.20) | copy-start | bytes 5505028
  6.5 48.4 %all-gather.11.cloned.1.call-start = ((), (), s32[]{:S(2)}) async-start(), calls=%async_computation.4 | async-start | bytes 1114112 | tf_op jit(solution)/shard_map/all_gather | solution.py:136
  7.3 78.6 %all-gather.7.cloned.1.call-start = ((), (), s32[]{:S(2)}) async-start(), calls=%async_computation.2 | async-start | bytes 4128768 | tf_op jit(solution)/shard_map/all_gather | solution.py:121
  8.0 146.3 %all-gather.5.cloned.1.call-start = ((), (), s32[]{:S(2)}) async-start(), calls=%async_computation.1 | async-start | bytes 4456448 | tf_op jit(solution)/shard_map/all_gather | solution.py:172
  8.7 186.5 %all-gather.9.cloned.1.call-start = ((), (), s32[]{:S(2)}) async-start(), calls=%async_computation.3 | async-start | bytes 4456448 | tf_op jit(solution)/shard_map/all_gather | solution.py:171
  9.3 238.1 %reduce-scatter.2.cloned.1.call-start = ((), (), s32[]{:S(2)}) async-start(), calls=%async_computation.5 | async-start | bytes 4128768 | tf_op jit(solution)/shard_map/reduce_scatter | solution.py:195
  53.4 35.5 %copy-start.10 = (f32[3584]{0:T(1024)S(1)}, f32[3584]{0:T(1024)}, u32[]{:S(2)}) copy-start(f32[3584]{0:T(1024)} %param.17) | copy-start | bytes 43012
  85.8 3.1 %copy-start.1 = (bf16[512,3584]{0,1:T(8,128)(2,1)S(1)}, bf16[512,3584]{0,1:T(8,128)(2,1)}, u32[]{:S(2)}) copy-start(bf16[512,3584]{0,1:T(8,128)(2,1)} %all-gather.7.cloned.1.call-done) | copy-start | bytes 11010052
  90.5 1.8 copy-start.2
  96.1 54.6 %collective-permute-start = (bf16[512,256]{1,0:T(8,128)(2,1)}, bf16[512,256]{1,0:T(8,128)(2,1)}, u32[]{:S(2)}, u32[]{:S(2)}) collective-permute-start(bf16[512,256]{1,0:T(8,128)(2,1)} %convolution_convert_fusion.1), channel_id=1, source_target_pairs={{0,8},{8,16},{16,24},{24,32},{32,40},{40,48},{48,56},{56,64},{64,7... | collective-permute-start | bytes 786440 | tf_op jit(solution)/shard_map/ppermute | solution.py:14
  107.7 44.8 %collective-permute-start.1 = (bf16[512,256]{0,1:T(8,128)(2,1)}, bf16[512,256]{0,1:T(8,128)(2,1)}, u32[]{:S(2)}, u32[]{:S(2)}) collective-permute-start(bf16[512,256]{0,1:T(8,128)(2,1)} %maximum_bitcast_fusion.6), channel_id=1, source_target_pairs={{0,8},{8,16},{16,24},{24,32},{32,40},{40,48},{48,56},{56,64},{64,7... | collective-permute-start | bytes 786440 | tf_op jit(solution)/shard_map/ppermute | solution.py:14
  160.0 40.1 %copy-start.5 = (bf16[512,256]{1,0:T(8,128)(2,1)S(1)}, bf16[512,256]{1,0:T(8,128)(2,1)}, u32[]{:S(2)}) copy-start(bf16[512,256]{1,0:T(8,128)(2,1)} %copy.52) | copy-start | bytes 786436
  160.0 40.1 %copy-start.7 = (bf16[512,256]{1,0:T(8,128)(2,1)S(1)}, bf16[512,256]{1,0:T(8,128)(2,1)}, u32[]{:S(2)}) copy-start(bf16[512,256]{1,0:T(8,128)(2,1)} %copy.51) | copy-start | bytes 786436
  195.3 4.8 %copy-start.8 = (bf16[512,2,128]{2,0,1:T(8,128)(2,1)S(1)}, bf16[512,2,128]{2,0,1:T(8,128)(2,1)}, u32[]{:S(2)}) copy-start(bf16[512,2,128]{2,0,1:T(8,128)(2,1)} %get-tuple-element.12) | copy-start | bytes 786436
  195.3 4.8 %copy-start.9 = (bf16[512,2,128]{2,0,1:T(8,128)(2,1)S(1)}, bf16[512,2,128]{2,0,1:T(8,128)(2,1)}, u32[]{:S(2)}) copy-start(bf16[512,2,128]{2,0,1:T(8,128)(2,1)} %get-tuple-element.13) | copy-start | bytes 786436
  201.9 2.2 copy-start.3
  201.9 2.2 copy-start.4
  201.9 2.2 copy-start.6
  204.2 2.8 %copy-start.11 = (bf16[512,3584]{1,0:T(8,128)(2,1)S(1)}, bf16[512,3584]{1,0:T(8,128)(2,1)}, u32[]{:S(2)}) copy-start(bf16[512,3584]{1,0:T(8,128)(2,1)} %param.21) | copy-start | bytes 11010052
Sparse Core Ops, SparseCore 0:
  9.5 45.3 all-gather.10
  56.6 29.1 all-gather.6
  88.0 53.9 all-gather.4
  144.0 51.2 all-gather.8
  211.0 36.3 reduce-scatter.1
where the time goes:
time: 255 us; the launch traced here: 254 us
  waiting for transfers between devices  104 us (41%)
  blocking collectives  52.9 us (21%)
  matrix products  33.9 us (13%)
  local copies, waits for them, and re-layouts  21.9 us (9%)
  other arithmetic  17.3 us (7%)
  between operations  16.1 us (6%)
  starting transfers between devices  7.77 us (3%)
    reduce_scatter x1, waiting for transfers between devices, on_device(): lax.psum_scatter(partial_out.astype(jnp.bfloat16), 'mp', scatter_dimensio...  36.5 us
    all_gather x1, waiting for transfers between devices, on_device(): lax.all_gather(cached_rotated_keys, 'group', axis=0, tiled=True)  35.3 us
    all_gather x1, waiting for transfers between devices, on_device(): whole = lax.all_gather(stream, 'mp', axis=1, tiled=True)  28.5 us
    all_gather x1, blocking collectives, on_device(): lax.all_gather(adapter_down_rows, 'group', axis=0, tiled=True)  26.9 us
    psum x1, blocking collectives, on_device(): low = lax.psum(partial_low, 'mp').astype(jnp.bfloat16)  26 us
    ppermute x2, starting transfers between devices, shifted(): lax.ppermute(value, axis, [(source, source + steps) for source in range(f...  7.62 us
    unnamed x27, local copies, waits for them, and re-layouts  5.37 us
    dot_general x1, matrix products, on_device(): jnp.dot(normalized_input, query_weight, preferred_element_type=jnp.float32)  5.26 us
  transfers between devices with their start and end apart: 7, of which 4 were waited for; matrix products, arithmetic and copies ran while one was open for 22% of the time, Pallas kernels for 0%

commit v1 on v0

--- a/solution.py
+++ b/solution.py
@@ -1,3 +1,4 @@
+import functools
 import jax
 import jax.numpy as jnp
 from jax import lax
@@ -6,6 +7,13 @@
 HEAD_WIDTH = 256
 REQS = 4
 adapter_scale = 2.0
+
+
+def render_targets(w_in, along_axis):
+    return jnp.sum(jax.lax.all_gather(w_in, along_axis), axis=0)
+
+
+push_views = functools.partial(render_targets, along_axis="mp")
 
 
 def shifted(value, axis, steps):
@@ -145,7 +153,7 @@
     partial_low = jnp.einsum(
         "td,rkd->trk", normed_part, chosen_down, preferred_element_type=jnp.float32
     ).reshape(count, REQS * rank_index)
-    low = lax.psum(partial_low, "mp").astype(jnp.bfloat16)
+    low = push_views(partial_low).astype(jnp.bfloat16)
     own_columns = jnp.repeat(member, rank_index, axis=1).astype(jnp.bfloat16)
     query_update = jnp.dot(
         low * own_columns,

time: 255 us -> 286 us (1.12)
  waiting for transfers between devices: 104 us -> 163 us
  blocking collectives: 52.9 us -> 27.6 us
  local copies, waits for them, and re-layouts: 21.9 us -> 18.8 us
    all_gather x1, waiting for transfers between devices: 0.01 us -> 27.5 us  [on_device(): lax.all_gather(cached_value_rows, 'group', axis=0, tiled=True)]
    psum x1 -> x0, blocking collectives: 26 us -> none  [on_device(): low = lax.psum(partial_low, 'mp').astype(jnp.bfloat16)]
    all_gather x0 -> x1, waiting for transfers between devices: none -> 19.1 us  [render_targets(): return jnp.sum(jax.lax.all_gather(w_in, along_axis), axis=0)]
    all_gather x1, waiting for transfers between devices: 35.3 us -> 47.6 us  [on_device(): lax.all_gather(cached_rotated_keys, 'group', axis=0, tiled=True)]
  transfers between devices with their start and end apart: 7 -> 8, of which waited for: 4 -> 6; matrix products, arithmetic and copies ran while one was open for 22% -> 17% of each run, Pallas kernels for 0% -> 0%
where the time goes in v1:
time: 286 us; the launch traced here: 285 us
  waiting for transfers between devices  163 us (57%)
  matrix products  34.6 us (12%)
  blocking collectives  27.6 us (10%)
  local copies, waits for them, and re-layouts  18.8 us (7%)
  other arithmetic  16.8 us (6%)
  between operations  16.3 us (6%)
  starting transfers between devices  7.86 us (3%)
    all_gather x1, waiting for transfers between devices, on_device(): lax.all_gather(cached_rotated_keys, 'group', axis=0, tiled=True)  47.6 us
    reduce_scatter x1, waiting for transfers between devices, on_device(): lax.psum_scatter(partial_out.astype(jnp.bfloat16), 'mp', scatter_dimensio...  36.9 us
    all_gather x1, waiting for transfers between devices, on_device(): whole = lax.all_gather(stream, 'mp', axis=1, tiled=True)  28.4 us
    all_gather x1, blocking collectives, on_device(): lax.all_gather(adapter_down_rows, 'group', axis=0, tiled=True)  27.6 us
    all_gather x1, waiting for transfers between devices, on_device(): lax.all_gather(cached_value_rows, 'group', axis=0, tiled=True)  27.5 us
    all_gather x1, waiting for transfers between devices, render_targets(): return jnp.sum(jax.lax.all_gather(w_in, along_axis), axis=0)  19.1 us
    ppermute x2, starting transfers between devices, shifted(): lax.ppermute(value, axis, [(source, source + steps) for source in range(f...  7.66 us
  transfers between devices with their start and end apart: 8, of which 6 were waited for; matrix products, arithmetic and copies ran while one was open for 17% of the time, Pallas kernels for 0%

profile of v1, /device:TPU:0, one launch (start us, length us, event | category | flops | bytes accessed | tf_op | source)
XLA Modules:
  0.0 284.7 jit_solution(6269163223299927176)
XLA Ops:
  19.3 2.6 compare_select_fusion.1
  22.0 27.6 %all_gather.21 = bf16[64,16,448]{2,1,0:T(8,128)(2,1)S(1)} all-gather(bf16[4,16,448]{2,1,0:T(8,128)(2,1)} %param.22), channel_id=1, replica_groups=mesh['group'=16,'mp'=8] {'group'}, dimensions={0}, use_global_device_ids=true | all-gather | bytes 974848 | tf_op jit(solution)/shard_map/all_gather | solution.py:143
  50.1 1.8 multiply_cosine_fusion
  55.0 2.4 convolution_convert_fusion.2
  57.4 28.4 %all-gather.8.cloned.1.call-done = bf16[512,3584]{0,1:T(8,128)(2,1)} async-done(((bf16[512,448]{0,1:T(8,128)(2,1)}), bf16[512,3584]{0,1:T(8,128)(2,1)}) %all-gather.8.cloned.1.call-update) | async-done | bytes 3670032 | tf_op jit(solution)/shard_map/all_gather | solution.py:129
  85.8 3.0 %fusion.2 = f32[512]{0:T(512)S(1)} fusion(bf16[512,3584]{0,1:T(8,128)(2,1)} %all-gather.8.cloned.1.call-done), kind=kLoop, calls=%fused_computation.7 | loop fusion | flops 5504512 | bytes 3672064 | tf_op jit(solution)/shard_map/reduce_sum | solution.py:132
  90.5 1.9 convolution_convert_fusion.1
  92.4 3.5 %collective-permute-start = (bf16[512,256]{1,0:T(8,128)(2,1)}, bf16[512,256]{1,0:T(8,128)(2,1)S(1)}, u32[]{:S(2)}, u32[]{:S(2)}) collective-permute-start(bf16[512,256]{1,0:T(8,128)(2,1)} %convolution_convert_fusion.1), channel_id=1, source_target_pairs={{0,8},{8,16},{16,24},{24,32},{32,40},{40,48},{48,56},{56,64},{64,7... | collective-permute-start | bytes 786440 | tf_op jit(solution)/shard_map/ppermute | solution.py:22
  96.8 4.1 %convolution_bitcast_fusion.1 = f32[512,1,256]{0,2,1:T(8,128)S(1)} fusion(bf16[512,3584]{0,1:T(8,128)(2,1)} %copy-done.2, bf16[3584,256]{1,0:T(8,128)(2,1)} %param.19), kind=kOutput, calls=%fused_computation.27 | convolution fusion | flops 939524096 | bytes 6029312 | tf_op jit(solution)/shard_map/dot_general | solution.py:169
  102.1 4.2 %collective-permute-start.1 = (bf16[512,256]{0,1:T(8,128)(2,1)S(1)}, bf16[512,256]{0,1:T(8,128)(2,1)}, u32[]{:S(2)}, u32[]{:S(2)}) collective-permute-start(bf16[512,256]{0,1:T(8,128)(2,1)S(1)} %maximum_bitcast_fusion.6), channel_id=1, source_target_pairs={{0,8},{8,16},{16,24},{24,32},{32,40},{40,48},{48,56},{56,64},{64,7... | collective-permute-start | bytes 786440 | tf_op jit(solution)/shard_map/ppermute | solution.py:22
  106.3 3.1 %fusion.86 = f32[512,512]{0,1:T(8,128)} fusion(bf16[512,3584]{0,1:T(8,128)(2,1)S(1)} %copy-done.3, bf16[3584,512]{1,0:T(8,128)(2,1)S(1)} %copy-done.8), kind=kOutput, calls=%fused_computation.132 | convolution fusion | flops 1879048192 | bytes 8388608 | tf_op jit(solution)/shard_map/dot_general | solution.py:164
  109.5 1.8 copy.44
  113.0 1.8 copy.48
  114.8 27.5 %all-gather.6.cloned.1.call-done = bf16[32,256,256]{2,1,0:T(8,128)(2,1)} async-done(((bf16[2,256,256]{2,1,0:T(8,128)(2,1)}), bf16[32,256,256]{2,1,0:T(8,128)(2,1)}) %all-gather.6.cloned.1.call-update) | async-done | bytes 4194320 | tf_op jit(solution)/shard_map/all_gather | solution.py:180
  142.3 4.6 %fusion.19 = bf16[4,256,256]{2,0,1:T(4,128)(2,1)S(1)} fusion(bf16[32,256,256]{2,1,0:T(8,128)(2,1)} %all-gather.6.cloned.1.call-done, s32[4]{0:T(128)S(1)} %dynamic-slice_reduce_fusion.1), kind=kOutput, calls=%fused_computation.25 | convolution fusion | flops 17039488 | bytes 4718608 | tf_op jit(solution)/shard_map/rj,jcd->rcd/dot_general | solution.py:185
  148.0 47.6 %all-gather.10.cloned.1.call-done = bf16[32,256,256]{2,1,0:T(8,128)(2,1)} async-done(((bf16[2,256,256]{2,1,0:T(8,128)(2,1)}), bf16[32,256,256]{2,1,0:T(8,128)(2,1)}) %all-gather.10.cloned.1.call-update) | async-done | bytes 4194320 | tf_op jit(solution)/shard_map/all_gather | solution.py:179
  195.6 4.6 %fusion.22 = bf16[4,256,256]{2,0,1:T(4,128)(2,1)S(1)} fusion(bf16[32,256,256]{2,1,0:T(8,128)(2,1)} %all-gather.10.cloned.1.call-done, s32[4]{0:T(128)S(1)} %dynamic-slice_reduce_fusion.1), kind=kOutput, calls=%fused_computation.26 | convolution fusion | flops 17039488 | bytes 4718608 | tf_op jit(solution)/shard_map/rj,jcd->rcd/dot_general | solution.py:184
  201.1 19.1 %all-gather.12.cloned.1.call-done = f32[8,512,64]{1,2,0:T(8,128)} async-done(((f32[1,512,64]{1,2,0:T(8,128)}), f32[8,512,64]{1,2,0:T(8,128)}) %all-gather.12.cloned.1.call-update) | async-done | bytes 1048592 | tf_op jit(solution)/shard_map/all_gather | solution.py:13
  225.3 2.0 copy.59
  228.7 3.5 %fusion.5 = (f32[2,512]{1,0:T(2,128)S(1)}, f32[2048,512,2]{1,0,2:T(8,128)S(1)}) fusion(pred[512,2048]{0,1:T(8,128)(4,1)S(1)} %pad_add_fusion, bf16[512,2,128]{2,0,1:T(8,128)(2,1)S(1)} %get-tuple-element.13, bf16[512,2,128]{2,0,1:T(8,128)(2,1)S(1)} %get-tuple-element.12, bf16[512,256]{1,0:T(8,128)(2,1)} %copy.49, bf16[512,256]{1,0:T(8,128)(2,1)} %copy.48, ...), kind=kOutput, calls=%fused_computation.10 | convolution fusion | flops 1084226560 | bytes 11014144 | tf_op jit(solution)/shard_map/tkrd,skd->krts/dot_general | solution.py:90
  232.3 2.0 fusion
  234.3 2.8 divide_convert_fusion
  237.1 3.9 %convolution_convert_fusion = bf16[512,3584]{0,1:T(8,128)(2,1)} fusion(bf16[512,512]{0,1:T(8,128)(2,1)S(1)} %bitcast.109, bf16[512,3584]{1,0:T(8,128)(2,1)S(1)} %copy-done.9), kind=kOutput, calls=%fused_computation.11 | convolution fusion | flops 1880883200 | bytes 7864320 | tf_op jit(solution)/shard_map/dot_general | solution.py:202
  241.0 36.9 %reduce-scatter.2.cloned.1.call-done = bf16[512,448]{0,1:T(8,128)(2,1)} async-done(((bf16[512,3584]{0,1:T(8,128)(2,1)}), bf16[512,448]{0,1:T(8,128)(2,1)}) %reduce-scatter.2.cloned.1.call-update) | async-done | bytes 458768 | tf_op jit(solution)/shard_map/reduce_scatter | solution.py:203
  (75 shorter events, 27.7 us)
Async XLA Ops:
  6.5 84.0 %copy-start = (bf16[3584,256]{1,0:T(8,128)(2,1)S(1)}, bf16[3584,256]{1,0:T(8,128)(2,1)}, u32[]{:S(2)}) copy-start(bf16[3584,256]{1,0:T(8,128)(2,1)} %param.20) | copy-start | bytes 5505028
  6.5 48.4 %all-gather.14.cloned.1.call-start = ((), (), s32[]{:S(2)}) async-start(), calls=%async_computation.5 | async-start | bytes 1114112 | tf_op jit(solution)/shard_map/all_gather | solution.py:144
  7.3 78.5 %all-gather.8.cloned.1.call-start = ((), (), s32[]{:S(2)}) async-start(), calls=%async_computation.2 | async-start | bytes 4128768 | tf_op jit(solution)/shard_map/all_gather | solution.py:129
  8.0 134.3 %all-gather.6.cloned.1.call-start = ((), (), s32[]{:S(2)}) async-start(), calls=%async_computation.1 | async-start | bytes 4456448 | tf_op jit(solution)/shard_map/all_gather | solution.py:180
  8.7 186.8 %all-gather.10.cloned.1.call-start = ((), (), s32[]{:S(2)}) async-start(), calls=%async_computation.3 | async-start | bytes 4456448 | tf_op jit(solution)/shard_map/all_gather | solution.py:179
  9.3 210.8 %all-gather.12.cloned.1.call-start = ((), (), s32[]{:S(2)}) async-start(), calls=%async_computation.4 | async-start | bytes 1179648 | tf_op jit(solution)/shard_map/all_gather | solution.py:13
  54.0 34.9 %copy-start.7 = (f32[3584]{0:T(1024)S(1)}, f32[3584]{0:T(1024)}, u32[]{:S(2)}) copy-start(f32[3584]{0:T(1024)} %param.17) | copy-start | bytes 43012
  85.8 3.1 %copy-start.1 = (bf16[512,3584]{0,1:T(8,128)(2,1)S(1)}, bf16[512,3584]{0,1:T(8,128)(2,1)}, u32[]{:S(2)}) copy-start(bf16[512,3584]{0,1:T(8,128)(2,1)} %all-gather.8.cloned.1.call-done) | copy-start | bytes 11010052
  90.5 5.4 %copy-start.2 = (bf16[512,3584]{0,1:T(8,128)(2,1)}, bf16[512,3584]{0,1:T(8,128)(2,1)S(1)}, u32[]{:S(2)}) copy-start(bf16[512,3584]{0,1:T(8,128)(2,1)S(1)} %fusion.4) | copy-start | bytes 11010052
  92.4 19.7 %collective-permute-start = (bf16[512,256]{1,0:T(8,128)(2,1)}, bf16[512,256]{1,0:T(8,128)(2,1)S(1)}, u32[]{:S(2)}, u32[]{:S(2)}) collective-permute-start(bf16[512,256]{1,0:T(8,128)(2,1)} %convolution_convert_fusion.1), channel_id=1, source_target_pairs={{0,8},{8,16},{16,24},{24,32},{32,40},{40,48},{48,56},{56,64},{64,7... | collective-permute-start | bytes 786440 | tf_op jit(solution)/shard_map/ppermute | solution.py:22
  96.8 181.1 %reduce-scatter.2.cloned.1.call-start = ((), (), s32[]{:S(2)}) async-start(), calls=%async_computation.6 | async-start | bytes 4128768 | tf_op jit(solution)/shard_map/reduce_scatter | solution.py:203
  96.8 9.5 %copy-start.3 = (bf16[512,3584]{0,1:T(8,128)(2,1)S(1)}, bf16[512,3584]{0,1:T(8,128)(2,1)}, u32[]{:S(2)}) copy-start(bf16[512,3584]{0,1:T(8,128)(2,1)} %copy-done.2) | copy-start | bytes 11010052
  96.8 9.5 %copy-start.8 = (bf16[3584,512]{1,0:T(8,128)(2,1)S(1)}, bf16[3584,512]{1,0:T(8,128)(2,1)}, u32[]{:S(2)}) copy-start(bf16[3584,512]{1,0:T(8,128)(2,1)} %param.18) | copy-start | bytes 11010052
  102.1 10.8 %collective-permute-start.1 = (bf16[512,256]{0,1:T(8,128)(2,1)S(1)}, bf16[512,256]{0,1:T(8,128)(2,1)}, u32[]{:S(2)}, u32[]{:S(2)}) collective-permute-start(bf16[512,256]{0,1:T(8,128)(2,1)S(1)} %maximum_bitcast_fusion.6), channel_id=1, source_target_pairs={{0,8},{8,16},{16,24},{24,32},{32,40},{40,48},{48,56},{56,64},{64,7... | collective-permute-start | bytes 786440 | tf_op jit(solution)/shard_map/ppermute | solution.py:22
  232.2 2.0 copy-start.4
  232.2 2.0 copy-start.5
  232.2 2.0 copy-start.6
  234.3 2.8 copy-start.9
Sparse Core Ops, SparseCore 0:
  9.5 45.4 all-gather.13
  56.6 29.1 all-gather.7
  87.9 54.3 all-gather.5
  144.3 51.2 all-gather.9
  197.1 22.9 all-gather.11
  241.1 36.7 reduce-scatter.1
